TPU v7x, 128 devices: a whole 4x4x4 slice. The times are simulated.
128 devices in a mesh: ang: 4 (over y), pix: 32 (over x, z, core).
Axes of the slice: x: 4, y: 4, z: 4, core: 2. Of those that a mesh axis runs over, the one named last changes fastest.
Arguments:
- flats: float32 [256, 256, 4096], P(None, 'pix', 'ang'), may hold values from -60 to 60
- projections: float32 [128, 256, 4096], P('ang', None, 'pix'), may hold values from -60 to 60
- start_basis: float32 [256, 48], replicated, may hold values from -0.375 to 0.375
Outputs:
- corrected: float32 [128, 256, 4096], P('ang', None, 'pix')
All inputs are finite; a program needn't handle non-finite values.
Results may differ from a plain program's by a relative error of at most 0.0001.
Values sent between devices are 32-bit elements; how exact they have to be, the bound alone decides.
No kernel may reach another device: no remote copies, remote signals or barrier semaphores. Data moves between devices by JAX's collectives and lax.ppermute only.
A program may use at most 128 MiB of HBM per device.

v0:
```python
import jax
import jax.numpy as jnp
from jax import lax
from jax.sharding import PartitionSpec as P

SUBSPACE = 2
floor_value = 0.2


def orthonormal(grown):
    correlation = jnp.dot(grown.T, grown, precision=lax.Precision.HIGHEST)
    lower = jnp.linalg.cholesky(correlation)
    return jax.scipy.linalg.solve_triangular(lower, grown.T, lower=True).T


def solve_normal(normal, fit_rhs):
    factor = jnp.linalg.cholesky(normal)
    return jax.scipy.linalg.cho_solve((factor, True), fit_rhs.T).T


def shards(flats, projections, start_basis):
    frames_here, rows_dev, cols_dev = flats.shape
    npix = rows_dev * cols_dev * lax.axis_size("ang") * lax.axis_size("pix")
    mean_flat = jnp.mean(flats, axis=0)
    centered = (flats - mean_flat).reshape(frames_here, -1)
    local_gram = jnp.dot(centered, centered.T, precision=lax.Precision.HIGHEST)
    gram = lax.psum(local_gram, ("ang", "pix")) / npix
    basis = start_basis
    for turn in range(SUBSPACE):
        basis = orthonormal(jnp.dot(gram, basis, precision=lax.Precision.HIGHEST))
    eigen_flats = jnp.dot(basis.T, centered, precision=lax.Precision.HIGHEST)
    normal = jnp.dot(
        basis.T,
        jnp.dot(gram, basis, precision=lax.Precision.HIGHEST),
        precision=lax.Precision.HIGHEST,
    )
    eigen_count = eigen_flats.shape[0]
    tiles = lax.all_to_all(projections, "pix", split_axis=1, concat_axis=2, tiled=True)
    eigen_rows, mean_rows = (
        lax.all_gather(
            eigen_flats.reshape(eigen_count, rows_dev, cols_dev), "ang", axis=2, tiled=True
        ),
        lax.all_gather(mean_flat, "ang", axis=1, tiled=True),
    )
    angle_count = tiles.shape[0]
    frames = tiles.reshape(angle_count, -1)
    flat_row = mean_rows.reshape(1, -1)
    eigen_wide = eigen_rows.reshape(eigen_count, -1)
    partial_value = jnp.dot(frames - flat_row, eigen_wide.T, precision=lax.Precision.HIGHEST)
    fit_rhs = lax.psum(partial_value, "pix") / npix
    weights = solve_normal(normal, fit_rhs)
    estimate = flat_row + jnp.dot(weights, eigen_wide, precision=lax.Precision.HIGHEST)
    tiles_out = (frames / jnp.maximum(estimate, floor_value)).reshape(tiles.shape)
    result = lax.all_to_all(tiles_out, "pix", split_axis=2, concat_axis=1, tiled=True)
    return result


def solution(mesh):
    in_specs = (P(None, "pix", "ang"), P("ang", None, "pix"), P())
    out_specs = P("ang", None, "pix")
    return jax.shard_map(shards, mesh=mesh, in_specs=in_specs, out_specs=out_specs, check_vma=False)
```

profile of v0, /device:TPU:1, one launch (start us, length us, event | category | flops | bytes accessed | tf_op | source)
XLA Modules:
  0.0 571.3 jit_solution(11641598748296280)
XLA Ops:
  6.5 3.9 reduce_sum.9
  10.5 4.4 broadcast_subtract_fusion
  14.8 3.2 copy-done.2
  18.1 17.2 %fusion.7 = f32[256,256]{1,0:T(8,128)} fusion(f32[256,8,1024]{2,1,0:T(8,128)S(1)} %broadcast_subtract_fusion), kind=kOutput, calls=%fused_computation.10 | convolution fusion | flops 6442450944 | bytes 8650752 | tf_op jit(solution)/shard_map/dot_general | solution.py:26
  35.3 0.4 all-gather.2.cloned.1.call-start
  35.7 15.0 %copy.49 = f32[32,8,8,1024]{3,1,2,0:T(8,128)} copy(f32[32,8,8,1024]{3,2,1,0:T(8,128)} %bitcast.84) | data formatting | bytes 16777216
  50.8 9.2 %copy.41 = f32[8192,256]{1,0:T(8,128)} copy(f32[8192,256]{0,1:T(8,128)} %bitcast.88) | data formatting | bytes 16777216 | tf_op jit(solution)/shard_map/dot_general | solution.py:31
  59.9 120.3 %all-reduce.2.cloned.1.call-done = f32[256,256]{1,0:T(8,128)} async-done(((f32[256,256]{1,0:T(8,128)}), f32[256,256]{1,0:T(8,128)}) %all-reduce.2.cloned.1.call-update) | async-done | bytes 262160 | tf_op jit(solution)/shard_map/psum | solution.py:27
  180.2 1.3 fusion.14
  181.6 0.2 fusion.47
  181.8 4.4 cholesky.59
  186.3 0.6 compare_reduce_fusion.2
  186.9 0.7 fusion.25
  187.6 3.7 custom-call.14
  191.2 0.2 fusion.23
  191.5 1.3 fusion.12
  192.8 0.2 fusion.48
  193.1 4.4 cholesky.70
  197.5 0.6 compare_reduce_fusion.1
  198.1 0.7 fusion.26
  198.8 3.7 custom-call.15
  202.5 0.2 fusion.21
  202.7 12.2 %fusion.19 = f32[48,8,1024]{2,0,1:T(8,128)} fusion(f32[8,1024,256]{2,1,0:T(8,128)} %bitcast.87, f32[48,256]{1,0:T(8,128)S(1)} %fusion.21), kind=kOutput, calls=%fused_computation.20 | convolution fusion | flops 1207959552 | bytes 10010624 | tf_op jit(solution)/shard_map/dot_general | solution.py:31
  215.0 6.6 %copy.33 = f32[32,256,128]{2,0,1:T(8,128)} copy(f32[32,256,128]{2,1,0:T(8,128)} %param.7) | data formatting | bytes 8388608 | tf_op args[1]
  221.6 5.6 all-to-all-start
  227.2 11.0 %all_gather.6 = f32[8,4096]{1,0:T(8,128)S(1)} all-gather(f32[8,1024]{1,0:T(8,128)S(1)} %broadcast_multiply_fusion), channel_id=1, replica_groups=mesh['ang'=4,'pix'=32] {'ang'}, dimensions={1}, use_global_device_ids=true | all-gather | bytes 163840 | tf_op jit(solution)/shard_map/all_gather | solution.py:43
  238.2 0.4 fusion.10
  238.6 0.2 fusion.49
  238.9 4.4 cholesky.81
  243.3 0.7 compare_reduce_fusion
  244.0 0.7 fusion.27
  244.7 3.7 custom-call.12
  248.4 31.1 %all-to-all-done = f32[32,256,128]{2,0,1:T(8,128)} async-done(((f32[32,256,128]{2,0,1:T(8,128)}), f32[32,256,128]{2,0,1:T(8,128)}, u32[]{:S(2)}, u32[]{:S(2)}) %all-to-all-start) | async-done | bytes 4194336 | tf_op jit(solution)/shard_map/all_to_all | solution.py:38
  279.5 6.7 %copy.34 = f32[32,32,8,128]{3,1,2,0:T(8,128)} copy(f32[32,32,8,128]{3,0,2,1:T(8,128)} %bitcast) | data formatting | bytes 8388608 | tf_op jit(solution)/shard_map/all_to_all | solution.py:38
  286.2 6.6 %bitcast_subtract_fusion = f32[32,8,32,128]{3,2,1,0:T(8,128)} fusion(f32[8,32,128]{2,1,0:T(8,128)S(1)} %copy.40, f32[32,32,8,128]{3,0,2,1:T(8,128)} %bitcast), kind=kLoop, calls=%fused_computation.8 | loop fusion | flops 1048576 | bytes 8519680 | tf_op jit(solution)/shard_map/sub | solution.py:49
  292.8 3.3 copy.45
  296.2 2.7 copy-done.3
  298.8 7.2 %fusion.4 = f32[32,48]{1,0:T(8,128)S(1)} fusion(f32[48,32768]{1,0:T(8,128)S(1)} %bitcast.89, f32[4,8,256,128]{3,2,1,0:T(8,128)S(1)} %bitcast.91), kind=kOutput, calls=%fused_computation.5 | convolution fusion | flops 603979776 | bytes 10491904 | tf_op jit(solution)/shard_map/dot_general | solution.py:49
  306.0 120.0 %psum.15 = f32[32,48]{1,0:T(8,128)S(1)} all-reduce(f32[32,48]{1,0:T(8,128)S(1)} %fusion.4), channel_id=1, replica_groups=mesh['ang'=4,'pix'=32] {'pix'}, use_global_device_ids=true, to_apply=%region_4.7 | all-reduce | flops 1536 | bytes 12288 | tf_op jit(solution)/shard_map/psum | solution.py:50
  426.4 9.0 %fusion.1 = f32[32,32768]{1,0:T(8,128)S(1)} fusion(f32[48,32]{0,1:T(8,128)S(1)} %fusion.28, f32[48,32768]{1,0:T(8,128)} %bitcast.90, f32[4,8,256,128]{3,2,1,0:T(8,128)} %bitcast.94, f32[32768]{0:T(1024)S(1)} %bitcast.98), kind=kOutput, calls=%fused_computation.2 | convolution fusion | flops 607125504 | bytes 14817280 | tf_op jit(solution)/shard_map/dot_general | solution.py:52
  435.4 4.4 copy.50
  439.9 10.8 %copy.43 = f32[32,8,4096]{0,1,2:T(8,128)} copy(f32[32,8,4096]{2,1,0:T(8,128)} %bitcast.92) | data formatting | bytes 8388608 | tf_op jit(solution)/shard_map/reshape | solution.py:53
  450.7 16.0 %reshape.47 = f32[32,1,32768]{2,1,0:T(1,128)} reshape(f32[4096,8,32]{2,1,0:T(8,128)} %bitcast.85) | data formatting | bytes 8388608
  466.7 61.1 %all_to_all.33 = f32[32,1,32768]{2,1,0:T(1,128)} all-to-all(f32[32,1,32768]{2,1,0:T(1,128)} %reshape.47), channel_id=1, replica_groups=mesh['ang'=4,'pix'=32] {'pix'}, dimensions={0} | all-to-all | bytes 8388608 | tf_op jit(solution)/shard_map/all_to_all | solution.py:54
  527.8 0.5 broadcast.81
  528.3 13.7 %reduce.4 = f32[32,32768]{1,0:T(8,128)} reduce(f32[32,1,32768]{2,1,0:T(1,128)} %all_to_all.33, f32[]{:T(128)} %broadcast.81), dimensions={1}, to_apply=%all_to_all.27.reduce_sub_computation | reduce | bytes 8388612 | tf_op jit(solution)/shard_map/all_to_all | solution.py:54
  542.1 9.8 %reshape.48 = f32[4096,8,32]{2,1,0:T(8,128)} reshape(f32[32,32768]{1,0:T(8,128)} %reduce.4) | data formatting | bytes 8388608
  551.9 12.1 %copy.44 = f32[32,32,8,128]{3,2,1,0:T(8,128)} copy(f32[32,32,8,128]{0,2,3,1:T(8,128)} %bitcast.86) | data formatting | bytes 8388608 | tf_op jit(solution)/shard_map/all_to_all | solution.py:54
  (28 shorter events, 0.7 us)
Async XLA Ops:
  6.5 173.7 %copy-start = (f32[256,48]{0,1:T(8,128)S(1)}, f32[256,48]{0,1:T(8,128)}, u32[]{:S(2)}) copy-start(f32[256,48]{0,1:T(8,128)} %param.8) | copy-start | bytes 147460
  6.5 173.7 %all-reduce.2.cloned.1.call-start = ((), (), s32[]{:S(2)}) async-start(), calls=%async_computation.2 | async-start | bytes 524288 | tf_op jit(solution)/shard_map/psum | solution.py:27
  14.8 3.2 copy-start.2
  35.3 257.5 %all-gather.2.cloned.1.call-start = ((), (), s32[]{:S(2)}) async-start(), calls=%async_computation.3 | async-start | bytes 7864320 | tf_op jit(solution)/shard_map/all_gather | solution.py:40
  221.6 16.6 %copy-start.5 = (f32[256,256]{1,0:T(8,128)S(1)}, f32[256,256]{1,0:T(8,128)}, u32[]{:S(2)}) copy-start(f32[256,256]{1,0:T(8,128)} %all-reduce.2.cloned.1.call-done) | copy-start | bytes 786436
  221.6 57.9 %all-to-all-start = ((f32[32,256,128]{2,0,1:T(8,128)}), f32[32,256,128]{2,0,1:T(8,128)}, u32[]{:S(2)}, u32[]{:S(2)}) async-start(f32[32,256,128]{2,0,1:T(8,128)} %copy.33), calls=%async_computation | async-start | bytes 8388608 | tf_op jit(solution)/shard_map/all_to_all | solution.py:38
  292.8 6.0 %copy-start.4 = (f32[32,8,32,128]{3,2,1,0:T(8,128)S(1)}, f32[32,8,32,128]{3,2,1,0:T(8,128)}, u32[]{:S(2)}) copy-start(f32[32,8,32,128]{3,2,1,0:T(8,128)} %bitcast_subtract_fusion) | copy-start | bytes 12582916
  296.2 2.7 copy-start.3
  551.9 12.1 %copy-start.1 = (f32[256,48]{0,1:T(8,128)S(1)}, f32[256,48]{0,1:T(8,128)}, u32[]{:S(2)}) copy-start(f32[256,48]{0,1:T(8,128)} %param.8) | copy-start | bytes 147460
Sparse Core Ops, SparseCore 0:
  35.4 144.7 all-reduce.1
  215.1 64.1 all-gather.1
where the time goes:
time: 581 us; the launch traced here: 571 us
  blocking collectives  192 us (33%)
  waiting for transfers between devices  151 us (26%)
  local copies, waits for them, and re-layouts  101 us (17%)
  other arithmetic  56.9 us (10%)
  matrix products  49.9 us (9%)
  between operations  14.1 us (2%)
  starting transfers between devices  6.04 us (1%)
    psum x1, waiting for transfers between devices, shards(): gram = lax.psum(local_gram, ('ang', 'pix')) / npix  120 us
    psum x1, blocking collectives, shards(): fit_rhs = lax.psum(partial_value, 'pix') / npix  120 us
    all_to_all x1, blocking collectives, shards(): lax.all_to_all(tiles_out, 'pix', split_axis=2, concat_axis=1, tiled=True)  61.1 us
    unnamed x18, local copies, waits for them, and re-layouts  57.8 us
    all_to_all x1, waiting for transfers between devices, shards(): lax.all_to_all(projections, 'pix', split_axis=1, concat_axis=2, tiled=True)  31.1 us
    dot_general x1, matrix products, shards(): local_gram = jnp.dot(centered, centered.T, precision=lax.Precision.HIGHEST)  17.2 us
    all_to_all x1, other arithmetic, shards(): lax.all_to_all(tiles_out, 'pix', split_axis=2, concat_axis=1, tiled=True)  13.7 us
    all_to_all x2, local copies, waits for them, and re-layouts, shards(): lax.all_to_all(tiles_out, 'pix', split_axis=2, concat_axis=1, tiled=True)  12.6 us
  transfers between devices with their start and end apart: 3, of which 2 were waited for; matrix products, arithmetic and copies ran while one was open for 10% of the time, Pallas kernels for 0%

commit v1 on v0

--- a/solution.py
+++ b/solution.py
@@ -24,7 +24,7 @@
     mean_flat = jnp.mean(flats, axis=0)
     centered = (flats - mean_flat).reshape(frames_here, -1)
     local_gram = jnp.dot(centered, centered.T, precision=lax.Precision.HIGHEST)
-    gram = lax.psum(local_gram, ("ang", "pix")) / npix
+    gram = lax.psum(lax.psum(local_gram, "pix"), "ang") / npix
     basis = start_basis
     for turn in range(SUBSPACE):
         basis = orthonormal(jnp.dot(gram, basis, precision=lax.Precision.HIGHEST))

time: 581 us -> 587 us (1.010)
    psum x1 -> x2, waiting for transfers between devices: 120 us -> 122 us  [shards(): gram = lax.psum(lax.psum(local_gram, 'pix'), 'ang') / npix]
  transfers between devices with their start and end apart: 3 -> 4, of which waited for: 2 -> 3; matrix products, arithmetic and copies ran while one was open for 10% -> 9% of each run, Pallas kernels for 0% -> 0%
where the time goes in v1:
time: 587 us; the launch traced here: 577 us
  blocking collectives  192 us (33%)
  waiting for transfers between devices  153 us (26%)
  local copies, waits for them, and re-layouts  101 us (17%)
  other arithmetic  56.9 us (10%)
  matrix products  49.9 us (9%)
  between operations  13.8 us (2%)
  starting transfers between devices  10.5 us (2%)
    psum x2, waiting for transfers between devices, shards(): gram = lax.psum(lax.psum(local_gram, 'pix'), 'ang') / npix  122 us
    psum x1, blocking collectives, shards(): fit_rhs = lax.psum(partial_value, 'pix') / npix  120 us
    all_to_all x1, blocking collectives, shards(): lax.all_to_all(tiles_out, 'pix', split_axis=2, concat_axis=1, tiled=True)  61.1 us
    unnamed x18, local copies, waits for them, and re-layouts  57.8 us
    all_to_all x1, waiting for transfers between devices, shards(): lax.all_to_all(projections, 'pix', split_axis=1, concat_axis=2, tiled=True)  31.1 us
    dot_general x1, matrix products, shards(): local_gram = jnp.dot(centered, centered.T, precision=lax.Precision.HIGHEST)  17.2 us
    all_to_all x1, other arithmetic, shards(): lax.all_to_all(tiles_out, 'pix', split_axis=2, concat_axis=1, tiled=True)  13.7 us
    all_to_all x2, local copies, waits for them, and re-layouts, shards(): lax.all_to_all(tiles_out, 'pix', split_axis=2, concat_axis=1, tiled=True)  12.6 us
  transfers between devices with their start and end apart: 4, of which 3 were waited for; matrix products, arithmetic and copies ran while one was open for 9% of the time, Pallas kernels for 0%

profile of v1, /device:TPU:1, one launch (start us, length us, event | category | flops | bytes accessed | tf_op | source)
XLA Modules:
  0.0 576.7 jit_solution(3775558492290017511)
XLA Ops:
  6.5 3.9 reduce_sum.9
  10.5 4.4 broadcast_subtract_fusion
  14.8 3.2 copy-done.2
  18.1 17.2 %fusion.7 = f32[256,256]{1,0:T(8,128)} fusion(f32[256,8,1024]{2,1,0:T(8,128)S(1)} %broadcast_subtract_fusion), kind=kOutput, calls=%fused_computation.10 | convolution fusion | flops 6442450944 | bytes 8650752 | tf_op jit(solution)/shard_map/dot_general | solution.py:26
  35.3 104.8 %all-reduce.3.cloned.1.call-done = f32[256,256]{1,0:T(8,128)} async-done(((f32[256,256]{1,0:T(8,128)}), f32[256,256]{1,0:T(8,128)}) %all-reduce.3.cloned.1.call-update) | async-done | bytes 262160 | tf_op jit(solution)/shard_map/psum | solution.py:27
  140.2 0.4 all-gather.2.cloned.1.call-start
  140.6 15.0 %copy.49 = f32[32,8,8,1024]{3,1,2,0:T(8,128)} copy(f32[32,8,8,1024]{3,2,1,0:T(8,128)} %bitcast.84) | data formatting | bytes 16777216
  155.6 9.2 %copy.41 = f32[8192,256]{1,0:T(8,128)} copy(f32[8192,256]{0,1:T(8,128)} %bitcast.88) | data formatting | bytes 16777216 | tf_op jit(solution)/shard_map/dot_general | solution.py:31
  164.8 16.8 %all-reduce.5.cloned.1.call-done = f32[256,256]{1,0:T(8,128)} async-done(((f32[256,256]{1,0:T(8,128)}), f32[256,256]{1,0:T(8,128)}) %all-reduce.5.cloned.1.call-update) | async-done | bytes 262160 | tf_op jit(solution)/shard_map/psum | solution.py:27
  181.7 1.3 fusion.14
  183.0 0.2 fusion.47
  183.2 4.4 cholesky.59
  187.7 0.6 compare_reduce_fusion.2
  188.3 0.7 fusion.25
  189.0 3.7 custom-call.14
  192.6 0.2 fusion.23
  192.9 1.3 fusion.12
  194.5 4.4 cholesky.70
  198.9 0.6 compare_reduce_fusion.1
  199.5 0.7 fusion.26
  200.2 3.7 custom-call.15
  203.9 0.2 fusion.21
  204.1 12.2 %fusion.19 = f32[48,8,1024]{2,0,1:T(8,128)} fusion(f32[8,1024,256]{2,1,0:T(8,128)} %bitcast.87, f32[48,256]{1,0:T(8,128)S(1)} %fusion.21), kind=kOutput, calls=%fused_computation.20 | convolution fusion | flops 1207959552 | bytes 10010624 | tf_op jit(solution)/shard_map/dot_general | solution.py:31
  216.4 6.6 %copy.33 = f32[32,256,128]{2,0,1:T(8,128)} copy(f32[32,256,128]{2,1,0:T(8,128)} %param.7) | data formatting | bytes 8388608 | tf_op args[1]
  223.0 10.0 %all-to-all-start = ((f32[32,256,128]{2,0,1:T(8,128)}), f32[32,256,128]{2,0,1:T(8,128)}, u32[]{:S(2)}, u32[]{:S(2)}) async-start(f32[32,256,128]{2,0,1:T(8,128)} %copy.33), calls=%async_computation | async-start | bytes 8388608 | tf_op jit(solution)/shard_map/all_to_all | solution.py:38
  233.0 11.0 %all_gather.6 = f32[8,4096]{1,0:T(8,128)S(1)} all-gather(f32[8,1024]{1,0:T(8,128)S(1)} %broadcast_multiply_fusion), channel_id=1, replica_groups=mesh['ang'=4,'pix'=32] {'ang'}, dimensions={1}, use_global_device_ids=true | all-gather | bytes 163840 | tf_op jit(solution)/shard_map/all_gather | solution.py:43
  244.0 0.4 fusion.10
  244.4 0.2 fusion.49
  244.7 4.4 cholesky.81
  249.1 0.7 compare_reduce_fusion
  249.8 0.7 fusion.27
  250.5 3.7 custom-call.12
  254.2 31.1 %all-to-all-done = f32[32,256,128]{2,0,1:T(8,128)} async-done(((f32[32,256,128]{2,0,1:T(8,128)}), f32[32,256,128]{2,0,1:T(8,128)}, u32[]{:S(2)}, u32[]{:S(2)}) %all-to-all-start) | async-done | bytes 4194336 | tf_op jit(solution)/shard_map/all_to_all | solution.py:38
  285.2 6.7 %copy.34 = f32[32,32,8,128]{3,1,2,0:T(8,128)} copy(f32[32,32,8,128]{3,0,2,1:T(8,128)} %bitcast) | data formatting | bytes 8388608 | tf_op jit(solution)/shard_map/all_to_all | solution.py:38
  291.9 6.6 %bitcast_subtract_fusion = f32[32,8,32,128]{3,2,1,0:T(8,128)} fusion(f32[8,32,128]{2,1,0:T(8,128)S(1)} %copy.40, f32[32,32,8,128]{3,0,2,1:T(8,128)} %bitcast), kind=kLoop, calls=%fused_computation.8 | loop fusion | flops 1048576 | bytes 8519680 | tf_op jit(solution)/shard_map/sub | solution.py:49
  298.5 3.3 copy.45
  301.9 2.7 copy-done.3
  304.6 7.2 %fusion.4 = f32[32,48]{1,0:T(8,128)S(1)} fusion(f32[48,32768]{1,0:T(8,128)S(1)} %bitcast.89, f32[4,8,256,128]{3,2,1,0:T(8,128)S(1)} %bitcast.91), kind=kOutput, calls=%fused_computation.5 | convolution fusion | flops 603979776 | bytes 10491904 | tf_op jit(solution)/shard_map/dot_general | solution.py:49
  311.7 120.0 %psum.23 = f32[32,48]{1,0:T(8,128)S(1)} all-reduce(f32[32,48]{1,0:T(8,128)S(1)} %fusion.4), channel_id=1, replica_groups=mesh['ang'=4,'pix'=32] {'pix'}, use_global_device_ids=true, to_apply=%region_5.8 | all-reduce | flops 1536 | bytes 12288 | tf_op jit(solution)/shard_map/psum | solution.py:50
  432.1 9.0 %fusion.1 = f32[32,32768]{1,0:T(8,128)S(1)} fusion(f32[48,32]{0,1:T(8,128)S(1)} %fusion.28, f32[48,32768]{1,0:T(8,128)} %bitcast.90, f32[4,8,256,128]{3,2,1,0:T(8,128)} %bitcast.94, f32[32768]{0:T(1024)S(1)} %bitcast.98), kind=kOutput, calls=%fused_computation.2 | convolution fusion | flops 607125504 | bytes 14817280 | tf_op jit(solution)/shard_map/dot_general | solution.py:52
  441.1 4.4 copy.50
  445.6 10.8 %copy.43 = f32[32,8,4096]{0,1,2:T(8,128)} copy(f32[32,8,4096]{2,1,0:T(8,128)} %bitcast.92) | data formatting | bytes 8388608 | tf_op jit(solution)/shard_map/reshape | solution.py:53
  456.4 16.0 %reshape.47 = f32[32,1,32768]{2,1,0:T(1,128)} reshape(f32[4096,8,32]{2,1,0:T(8,128)} %bitcast.85) | data formatting | bytes 8388608
  472.4 61.1 %all_to_all.33 = f32[32,1,32768]{2,1,0:T(1,128)} all-to-all(f32[32,1,32768]{2,1,0:T(1,128)} %reshape.47), channel_id=1, replica_groups=mesh['ang'=4,'pix'=32] {'pix'}, dimensions={0} | all-to-all | bytes 8388608 | tf_op jit(solution)/shard_map/all_to_all | solution.py:54
  533.5 0.5 broadcast.81
  534.1 13.7 %reduce.4 = f32[32,32768]{1,0:T(8,128)} reduce(f32[32,1,32768]{2,1,0:T(1,128)} %all_to_all.33, f32[]{:T(128)} %broadcast.81), dimensions={1}, to_apply=%all_to_all.27.reduce_sub_computation | reduce | bytes 8388612 | tf_op jit(solution)/shard_map/all_to_all | solution.py:54
  547.8 9.8 %reshape.48 = f32[4096,8,32]{2,1,0:T(8,128)} reshape(f32[32,32768]{1,0:T(8,128)} %reduce.4) | data formatting | bytes 8388608
  557.6 12.1 %copy.44 = f32[32,32,8,128]{3,2,1,0:T(8,128)} copy(f32[32,32,8,128]{0,2,3,1:T(8,128)} %bitcast.86) | data formatting | bytes 8388608 | tf_op jit(solution)/shard_map/all_to_all | solution.py:54
  (31 shorter events, 1.0 us)
Async XLA Ops:
  6.5 175.1 %copy-start = (f32[256,48]{0,1:T(8,128)S(1)}, f32[256,48]{0,1:T(8,128)}, u32[]{:S(2)}) copy-start(f32[256,48]{0,1:T(8,128)} %param.8) | copy-start | bytes 147460
  6.5 133.6 %all-reduce.3.cloned.1.call-start = ((), (), s32[]{:S(2)}) async-start(), calls=%async_computation.2 | async-start | bytes 524288 | tf_op jit(solution)/shard_map/psum | solution.py:27
  14.8 3.2 copy-start.2
  35.3 146.4 %all-reduce.5.cloned.1.call-start = ((), (), s32[]{:S(2)}) async-start(), calls=%async_computation.3 | async-start | bytes 524288 | tf_op jit(solution)/shard_map/psum | solution.py:27
  140.2 158.4 %all-gather.2.cloned.1.call-start = ((), (), s32[]{:S(2)}) async-start(), calls=%async_computation.4 | async-start | bytes 7864320 | tf_op jit(solution)/shard_map/all_gather | solution.py:40
  223.0 21.0 %copy-start.5 = (f32[256,256]{1,0:T(8,128)S(1)}, f32[256,256]{1,0:T(8,128)}, u32[]{:S(2)}) copy-start(f32[256,256]{1,0:T(8,128)} %all-reduce.5.cloned.1.call-done) | copy-start | bytes 786436
  223.0 62.2 %all-to-all-start = ((f32[32,256,128]{2,0,1:T(8,128)}), f32[32,256,128]{2,0,1:T(8,128)}, u32[]{:S(2)}, u32[]{:S(2)}) async-start(f32[32,256,128]{2,0,1:T(8,128)} %copy.33), calls=%async_computation | async-start | bytes 8388608 | tf_op jit(solution)/shard_map/all_to_all | solution.py:38
  298.5 6.0 %copy-start.4 = (f32[32,8,32,128]{3,2,1,0:T(8,128)S(1)}, f32[32,8,32,128]{3,2,1,0:T(8,128)}, u32[]{:S(2)}) copy-start(f32[32,8,32,128]{3,2,1,0:T(8,128)} %bitcast_subtract_fusion) | copy-start | bytes 12582916
  301.9 2.7 copy-start.3
  557.6 12.1 %copy-start.1 = (f32[256,48]{0,1:T(8,128)S(1)}, f32[256,48]{0,1:T(8,128)}, u32[]{:S(2)}) copy-start(f32[256,48]{0,1:T(8,128)} %param.8) | copy-start | bytes 147460
Sparse Core Ops, SparseCore 0:
  35.4 104.6 all-reduce.2
  142.6 39.0 all-reduce.4
  216.5 69.2 all-gather.1
